TPU v7x, 512 devices: a whole 4x4x16 slice. The times are simulated.
512 devices in a mesh: px: 32 (over y, x, core), py: 16 (over z).
Axes of the slice: x: 4, y: 4, z: 16, core: 2. Of those that a mesh axis runs over, the one named last changes fastest.
Arguments:
- start_vecs: float32 [8192, 64, 128], P(('px', 'py')), may hold values from -6 to 6
- local_tiles: bfloat16 [8192, 4, 128, 128], P(('px', 'py')), may hold values from -0.078125 to 0.078125
- local_cols: int32 [8192, 4], P(('px', 'py')), may hold values from 0 to 15
- halo_tiles: bfloat16 [8192, 128, 128], P(('px', 'py')), may hold values from -0.078125 to 0.078125
- halo_slot: int32 [8192], P(('px', 'py')), may hold values from 0 to 7
- boundary: int32 [2048, 2], P(('px', 'py')), may hold values from 0 to 15
Outputs:
- filtered: float32 [8192, 64, 128], P(('px', 'py'))
- gram_matrix: float32 [64, 64], replicated
Inputs may be any that keep to these rules, and one draw needn't show every extreme that they name: `local_cols`: local block indices within the partition. `boundary`: local block indices within the partition.
All inputs are finite; a program needn't handle non-finite values.
Results may differ from a plain program's by a relative error of at most 0.0055.
Values may be sent and summed in bfloat16 or wider, within the bound.
No kernel may reach another device: no remote copies, remote signals or barrier semaphores. Data moves between devices by JAX's collectives and lax.ppermute only.
A program may use at most 64 MiB of HBM per device.

v0:
```python
import jax
import jax.numpy as jnp
from jax import lax
from jax.sharding import PartitionSpec as P

DEG = 9


def from_behind(value, axis, steps):
    count = lax.axis_size(axis)
    pairs = [(source, (source + steps) % count) for source in range(count)]
    return lax.ppermute(value, axis, pairs)


def operator_apply(current, local_tiles, local_cols, halo_tiles, halo_slot, boundary):
    rounded = current.astype(jnp.bfloat16)
    outgoing = rounded[boundary]
    from_xlow = from_behind(outgoing[0], "px", 1)
    from_xhigh = from_behind(outgoing[1], "px", -1)
    from_ylow = from_behind(outgoing[2], "py", 1)
    from_yhigh = from_behind(outgoing[3], "py", -1)
    received = jnp.concatenate([from_xlow, from_xhigh, from_ylow, from_yhigh], axis=0)
    gathered = rounded[local_cols]
    product = jnp.einsum(
        "rtkj,rtij->rki", gathered, local_tiles, preferred_element_type=jnp.float32
    )
    coupled = jnp.einsum(
        "rkj,rij->rki", received[halo_slot], halo_tiles, preferred_element_type=jnp.float32
    )
    return product + coupled


def shards(start_vecs, local_tiles, local_cols, halo_tiles, halo_slot, boundary):

    def step_apply(current):
        return operator_apply(current, local_tiles, local_cols, halo_tiles, halo_slot, boundary)

    first_vecs = step_apply(start_vecs)

    def advance(step_index, state_pair):
        older_vec, newer_vec = state_pair
        return (newer_vec, 2.0 * step_apply(newer_vec) - older_vec)

    previous, current = lax.fori_loop(0, DEG - 1, advance, (start_vecs, first_vecs))
    total_rows = current.shape[0] * current.shape[2] * lax.axis_size("px") * lax.axis_size("py")
    squares = lax.psum(jnp.sum(current * current, axis=(0, 2)), ("px", "py"))
    scales = lax.rsqrt(squares / total_rows + 1e-06)
    filtered = current * scales[None, :, None]
    partial_gram = jnp.einsum("rkj,rlj->kl", filtered, filtered, precision=lax.Precision.HIGHEST)
    gram_matrix = lax.psum(partial_gram, ("px", "py")) / total_rows
    return (filtered, gram_matrix)


def solution(mesh):
    return jax.shard_map(
        shards,
        mesh=mesh,
        in_specs=(
            P(("px", "py"), None, None),
            P(("px", "py"), None, None, None),
            P(("px", "py"), None),
            P(("px", "py"), None, None),
            P(("px", "py")),
            P(("px", "py"), None),
        ),
        out_specs=(P(("px", "py"), None, None), P()),
        check_vma=False,
    )
```

profile of v0, /device:TPU:1, one launch (start us, length us, event | category | flops | bytes accessed | tf_op | source)
XLA Modules:
  0.0 419.5 jit_solution(5818227597087407548)
XLA Ops:
  0.7 1.2 copy.33
  3.4 4.5 %collective-permute-start.4 = (bf16[2,64,128]{2,1,0:T(8,128)(2,1)S(1)}, bf16[2,64,128]{2,1,0:T(8,128)(2,1)S(1)}, u32[]{:S(2)}, u32[]{:S(2)}) collective-permute-start(bf16[2,64,128]{2,1,0:T(8,128)(2,1)S(1)} %get-tuple-element.65), channel_id=1, source_target_pairs={{0,16},{16,32},{32,48},{48,64},{64,80},{80,96},{96,112},{112,128},... | collective-permute-start | bytes 98312 | tf_op jit(solution)/shard_map/ppermute | solution.py:12
  7.9 3.5 collective-permute-start.6
  11.4 4.5 %collective-permute-start.5 = (bf16[2,64,128]{2,1,0:T(8,128)(2,1)S(1)}, bf16[2,64,128]{2,1,0:T(8,128)(2,1)S(1)}, u32[]{:S(2)}, u32[]{:S(2)}) collective-permute-start(bf16[2,64,128]{2,1,0:T(8,128)(2,1)S(1)} %get-tuple-element.67), channel_id=1, source_target_pairs={{0,496},{16,0},{32,16},{48,32},{64,48},{80,64},{96,80},{112,96},{1... | collective-permute-start | bytes 98312 | tf_op jit(solution)/shard_map/ppermute | solution.py:12
  16.0 6.9 %collective-permute-start.7 = (bf16[2,64,128]{2,1,0:T(8,128)(2,1)S(1)}, bf16[2,64,128]{2,1,0:T(8,128)(2,1)S(1)}, u32[]{:S(2)}, u32[]{:S(2)}) collective-permute-start(bf16[2,64,128]{2,1,0:T(8,128)(2,1)S(1)} %get-tuple-element.68), channel_id=1, source_target_pairs={{0,15},{1,0},{2,1},{3,2},{4,3},{5,4},{6,5},{7,6},{8,7},{9,8},{10,9... | collective-permute-start | bytes 98312 | tf_op jit(solution)/shard_map/ppermute | solution.py:12
  23.1 1.7 gather_fusion.3
  24.8 2.9 convolution_bitcast_fusion.1
  28.4 1.5 convolution_add_fusion.1
  29.9 184.2 %while.12 = (s32[]{:T(128)}, f32[16,64,128]{2,1,0:T(8,128)}, f32[16,64,128]{2,1,0:T(8,128)S(1)}, s32[16,4]{0,1:T(4,128)S(1)}, bf16[16,4,128,128]{3,2,1,0:T(8,128...) while((s32[]{:T(128)}, f32[16,64,128]{2,1,0:T(8,128)}, ...), condition=%wide.region_1.0_spmd, body=%wide.region_0.0_spmd.sunk | while | flops 168496400 | bytes 23345988 | solution.py:44
  30.8 3.4 collective-permute-start
  34.1 1.9 collective-permute-start.1
  36.1 6.7 %collective-permute-start.2 = (bf16[2,64,128]{2,1,0:T(8,128)(2,1)S(1)}, bf16[2,64,128]{2,1,0:T(8,128)(2,1)S(1)}, u32[]{:S(2)}, u32[]{:S(2)}) collective-permute-start(bf16[2,64,128]{2,1,0:T(8,128)(2,1)S(1)} %get-tuple-element.124), channel_id=1, source_target_pairs={{0,496},{16,0},{32,16},{48,32},{64,48},{80,64},{96,80},{112,96},{1... | collective-permute-start | bytes 98312 | tf_op jit(solution)/shard_map/while/body/eval_jaxpr/ppermute | solution.py:12
  42.8 1.9 collective-permute-start.3
  45.7 2.4 convolution_bitcast_fusion.4
  48.8 1.8 fusion.28
  50.6 0.8 copy.29
  52.7 4.6 %collective-permute-start = (bf16[2,64,128]{2,1,0:T(8,128)(2,1)S(1)}, bf16[2,64,128]{2,1,0:T(8,128)(2,1)S(1)}, u32[]{:S(2)}, u32[]{:S(2)}) collective-permute-start(bf16[2,64,128]{2,1,0:T(8,128)(2,1)S(1)} %get-tuple-element.122), channel_id=1, source_target_pairs={{0,15},{1,0},{2,1},{3,2},{4,3},{5,4},{6,5},{7,6},{8,7},{9,8},{10,9... | collective-permute-start | bytes 98312 | tf_op jit(solution)/shard_map/while/body/eval_jaxpr/ppermute | solution.py:12
  57.3 1.9 collective-permute-start.1
  59.2 5.4 %collective-permute-start.2 = (bf16[2,64,128]{2,1,0:T(8,128)(2,1)S(1)}, bf16[2,64,128]{2,1,0:T(8,128)(2,1)S(1)}, u32[]{:S(2)}, u32[]{:S(2)}) collective-permute-start(bf16[2,64,128]{2,1,0:T(8,128)(2,1)S(1)} %get-tuple-element.124), channel_id=1, source_target_pairs={{0,496},{16,0},{32,16},{48,32},{64,48},{80,64},{96,80},{112,96},{1... | collective-permute-start | bytes 98312 | tf_op jit(solution)/shard_map/while/body/eval_jaxpr/ppermute | solution.py:12
  64.6 1.9 collective-permute-start.3
  67.5 2.4 convolution_bitcast_fusion.4
  70.6 1.8 fusion.28
  72.4 0.8 copy.29
  74.5 4.9 %collective-permute-start = (bf16[2,64,128]{2,1,0:T(8,128)(2,1)S(1)}, bf16[2,64,128]{2,1,0:T(8,128)(2,1)S(1)}, u32[]{:S(2)}, u32[]{:S(2)}) collective-permute-start(bf16[2,64,128]{2,1,0:T(8,128)(2,1)S(1)} %get-tuple-element.122), channel_id=1, source_target_pairs={{0,15},{1,0},{2,1},{3,2},{4,3},{5,4},{6,5},{7,6},{8,7},{9,8},{10,9... | collective-permute-start | bytes 98312 | tf_op jit(solution)/shard_map/while/body/eval_jaxpr/ppermute | solution.py:12
  79.4 1.9 collective-permute-start.1
  81.3 6.7 %collective-permute-start.2 = (bf16[2,64,128]{2,1,0:T(8,128)(2,1)S(1)}, bf16[2,64,128]{2,1,0:T(8,128)(2,1)S(1)}, u32[]{:S(2)}, u32[]{:S(2)}) collective-permute-start(bf16[2,64,128]{2,1,0:T(8,128)(2,1)S(1)} %get-tuple-element.124), channel_id=1, source_target_pairs={{0,496},{16,0},{32,16},{48,32},{64,48},{80,64},{96,80},{112,96},{1... | collective-permute-start | bytes 98312 | tf_op jit(solution)/shard_map/while/body/eval_jaxpr/ppermute | solution.py:12
  88.0 1.9 collective-permute-start.3
  90.9 2.4 convolution_bitcast_fusion.4
  94.0 1.8 fusion.28
  95.9 0.8 copy.29
  97.9 4.8 %collective-permute-start = (bf16[2,64,128]{2,1,0:T(8,128)(2,1)S(1)}, bf16[2,64,128]{2,1,0:T(8,128)(2,1)S(1)}, u32[]{:S(2)}, u32[]{:S(2)}) collective-permute-start(bf16[2,64,128]{2,1,0:T(8,128)(2,1)S(1)} %get-tuple-element.122), channel_id=1, source_target_pairs={{0,15},{1,0},{2,1},{3,2},{4,3},{5,4},{6,5},{7,6},{8,7},{9,8},{10,9... | collective-permute-start | bytes 98312 | tf_op jit(solution)/shard_map/while/body/eval_jaxpr/ppermute | solution.py:12
  102.8 1.9 collective-permute-start.1
  104.7 6.7 %collective-permute-start.2 = (bf16[2,64,128]{2,1,0:T(8,128)(2,1)S(1)}, bf16[2,64,128]{2,1,0:T(8,128)(2,1)S(1)}, u32[]{:S(2)}, u32[]{:S(2)}) collective-permute-start(bf16[2,64,128]{2,1,0:T(8,128)(2,1)S(1)} %get-tuple-element.124), channel_id=1, source_target_pairs={{0,496},{16,0},{32,16},{48,32},{64,48},{80,64},{96,80},{112,96},{1... | collective-permute-start | bytes 98312 | tf_op jit(solution)/shard_map/while/body/eval_jaxpr/ppermute | solution.py:12
  111.4 1.9 collective-permute-start.3
  114.3 2.4 convolution_bitcast_fusion.4
  117.4 1.8 fusion.28
  121.3 4.9 %collective-permute-start = (bf16[2,64,128]{2,1,0:T(8,128)(2,1)S(1)}, bf16[2,64,128]{2,1,0:T(8,128)(2,1)S(1)}, u32[]{:S(2)}, u32[]{:S(2)}) collective-permute-start(bf16[2,64,128]{2,1,0:T(8,128)(2,1)S(1)} %get-tuple-element.122), channel_id=1, source_target_pairs={{0,15},{1,0},{2,1},{3,2},{4,3},{5,4},{6,5},{7,6},{8,7},{9,8},{10,9... | collective-permute-start | bytes 98312 | tf_op jit(solution)/shard_map/while/body/eval_jaxpr/ppermute | solution.py:12
  126.2 1.9 collective-permute-start.1
  128.1 6.7 %collective-permute-start.2 = (bf16[2,64,128]{2,1,0:T(8,128)(2,1)S(1)}, bf16[2,64,128]{2,1,0:T(8,128)(2,1)S(1)}, u32[]{:S(2)}, u32[]{:S(2)}) collective-permute-start(bf16[2,64,128]{2,1,0:T(8,128)(2,1)S(1)} %get-tuple-element.124), channel_id=1, source_target_pairs={{0,496},{16,0},{32,16},{48,32},{64,48},{80,64},{96,80},{112,96},{1... | collective-permute-start | bytes 98312 | tf_op jit(solution)/shard_map/while/body/eval_jaxpr/ppermute | solution.py:12
  134.8 1.9 collective-permute-start.3
  137.7 2.4 convolution_bitcast_fusion.4
  140.8 1.8 fusion.28
  142.7 0.8 copy.29
  144.7 4.8 %collective-permute-start = (bf16[2,64,128]{2,1,0:T(8,128)(2,1)S(1)}, bf16[2,64,128]{2,1,0:T(8,128)(2,1)S(1)}, u32[]{:S(2)}, u32[]{:S(2)}) collective-permute-start(bf16[2,64,128]{2,1,0:T(8,128)(2,1)S(1)} %get-tuple-element.122), channel_id=1, source_target_pairs={{0,15},{1,0},{2,1},{3,2},{4,3},{5,4},{6,5},{7,6},{8,7},{9,8},{10,9... | collective-permute-start | bytes 98312 | tf_op jit(solution)/shard_map/while/body/eval_jaxpr/ppermute | solution.py:12
  149.6 1.9 collective-permute-start.1
  151.5 6.7 %collective-permute-start.2 = (bf16[2,64,128]{2,1,0:T(8,128)(2,1)S(1)}, bf16[2,64,128]{2,1,0:T(8,128)(2,1)S(1)}, u32[]{:S(2)}, u32[]{:S(2)}) collective-permute-start(bf16[2,64,128]{2,1,0:T(8,128)(2,1)S(1)} %get-tuple-element.124), channel_id=1, source_target_pairs={{0,496},{16,0},{32,16},{48,32},{64,48},{80,64},{96,80},{112,96},{1... | collective-permute-start | bytes 98312 | tf_op jit(solution)/shard_map/while/body/eval_jaxpr/ppermute | solution.py:12
  158.2 1.9 collective-permute-start.3
  161.1 2.4 convolution_bitcast_fusion.4
  164.2 1.8 fusion.28
  166.1 0.8 copy.29
  168.2 4.9 %collective-permute-start = (bf16[2,64,128]{2,1,0:T(8,128)(2,1)S(1)}, bf16[2,64,128]{2,1,0:T(8,128)(2,1)S(1)}, u32[]{:S(2)}, u32[]{:S(2)}) collective-permute-start(bf16[2,64,128]{2,1,0:T(8,128)(2,1)S(1)} %get-tuple-element.122), channel_id=1, source_target_pairs={{0,15},{1,0},{2,1},{3,2},{4,3},{5,4},{6,5},{7,6},{8,7},{9,8},{10,9... | collective-permute-start | bytes 98312 | tf_op jit(solution)/shard_map/while/body/eval_jaxpr/ppermute | solution.py:12
  173.0 1.9 collective-permute-start.1
  174.9 6.7 %collective-permute-start.2 = (bf16[2,64,128]{2,1,0:T(8,128)(2,1)S(1)}, bf16[2,64,128]{2,1,0:T(8,128)(2,1)S(1)}, u32[]{:S(2)}, u32[]{:S(2)}) collective-permute-start(bf16[2,64,128]{2,1,0:T(8,128)(2,1)S(1)} %get-tuple-element.124), channel_id=1, source_target_pairs={{0,496},{16,0},{32,16},{48,32},{64,48},{80,64},{96,80},{112,96},{1... | collective-permute-start | bytes 98312 | tf_op jit(solution)/shard_map/while/body/eval_jaxpr/ppermute | solution.py:12
  181.6 1.9 collective-permute-start.3
  184.5 2.4 convolution_bitcast_fusion.4
  187.6 1.8 fusion.28
  191.6 4.8 %collective-permute-start = (bf16[2,64,128]{2,1,0:T(8,128)(2,1)S(1)}, bf16[2,64,128]{2,1,0:T(8,128)(2,1)S(1)}, u32[]{:S(2)}, u32[]{:S(2)}) collective-permute-start(bf16[2,64,128]{2,1,0:T(8,128)(2,1)S(1)} %get-tuple-element.122), channel_id=1, source_target_pairs={{0,15},{1,0},{2,1},{3,2},{4,3},{5,4},{6,5},{7,6},{8,7},{9,8},{10,9... | collective-permute-start | bytes 98312 | tf_op jit(solution)/shard_map/while/body/eval_jaxpr/ppermute | solution.py:12
  196.4 1.9 collective-permute-start.1
  198.3 6.7 %collective-permute-start.2 = (bf16[2,64,128]{2,1,0:T(8,128)(2,1)S(1)}, bf16[2,64,128]{2,1,0:T(8,128)(2,1)S(1)}, u32[]{:S(2)}, u32[]{:S(2)}) collective-permute-start(bf16[2,64,128]{2,1,0:T(8,128)(2,1)S(1)} %get-tuple-element.124), channel_id=1, source_target_pairs={{0,496},{16,0},{32,16},{48,32},{64,48},{80,64},{96,80},{112,96},{1... | collective-permute-start | bytes 98312 | tf_op jit(solution)/shard_map/while/body/eval_jaxpr/ppermute | solution.py:12
  205.0 1.9 collective-permute-start.3
  207.9 2.4 convolution_bitcast_fusion.4
  211.1 1.8 fusion.28
  214.3 105.2 %psum.14 = f32[64]{0:T(128)S(1)} all-reduce(f32[64]{0:T(128)S(1)} %multiply_reduce_fusion), channel_id=1, replica_groups=mesh['px'=32,'py'=16] {'px','py'}, use_global_device_ids=true, to_apply=%region_3.0 | all-reduce | flops 64 | bytes 512 | tf_op jit(solution)/shard_map/psum | solution.py:46
  320.2 98.6 %psum.15 = f32[64,64]{1,0:T(8,128)S(1)} all-reduce(f32[64,64]{1,0:T(8,128)S(1)} %convolution_bitcast_fusion.2), channel_id=1, replica_groups=mesh['px'=32,'py'=16] {'px','py'}, use_global_device_ids=true, to_apply=%region_4.0 | all-reduce | flops 4096 | bytes 32768 | tf_op jit(solution)/shard_map/psum | solution.py:50
  (241 shorter events, 28.7 us)
Async XLA Ops:
  0.6 24.1 %copy-start = (bf16[16,4,128,128]{3,2,1,0:T(8,128)(2,1)S(1)}, bf16[16,4,128,128]{3,2,1,0:T(8,128)(2,1)}, u32[]{:S(2)}) copy-start(bf16[16,4,128,128]{3,2,1,0:T(8,128)(2,1)} %param.9) | copy-start | bytes 6291460
  0.6 22.3 %copy-start.6 = (s32[16,4]{0,1:T(4,128)S(1)}, s32[16,4]{0,1:T(4,128)}, u32[]{:S(2)}) copy-start(s32[16,4]{0,1:T(4,128)} %param.10) | copy-start | bytes 772
  0.7 22.2 %copy-start.8 = (s32[16]{0:T(128)S(1)}, s32[16]{0:T(128)}, u32[]{:S(2)}) copy-start(s32[16]{0:T(128)} %param.12) | copy-start | bytes 196
  1.9 25.8 %copy-start.2 = (f32[16,64,128]{2,1,0:T(8,128)}, f32[16,64,128]{2,1,0:T(8,128)S(1)}, u32[]{:S(2)}) copy-start(f32[16,64,128]{2,1,0:T(8,128)S(1)} %copy.33) | copy-start | bytes 1572868
  3.4 24.3 %collective-permute-start.4 = (bf16[2,64,128]{2,1,0:T(8,128)(2,1)S(1)}, bf16[2,64,128]{2,1,0:T(8,128)(2,1)S(1)}, u32[]{:S(2)}, u32[]{:S(2)}) collective-permute-start(bf16[2,64,128]{2,1,0:T(8,128)(2,1)S(1)} %get-tuple-element.65), channel_id=1, source_target_pairs={{0,16},{16,32},{32,48},{48,64},{64,80},{80,96},{96,112},{112,128},... | collective-permute-start | bytes 98312 | tf_op jit(solution)/shard_map/ppermute | solution.py:12
  7.9 19.8 %collective-permute-start.6 = (bf16[2,64,128]{2,1,0:T(8,128)(2,1)S(1)}, bf16[2,64,128]{2,1,0:T(8,128)(2,1)S(1)}, u32[]{:S(2)}, u32[]{:S(2)}) collective-permute-start(bf16[2,64,128]{2,1,0:T(8,128)(2,1)S(1)} %get-tuple-element.66), channel_id=1, source_target_pairs={{0,1},{1,2},{2,3},{3,4},{4,5},{5,6},{6,7},{7,8},{8,9},{9,10},{10,1... | collective-permute-start | bytes 98312 | tf_op jit(solution)/shard_map/ppermute | solution.py:12
  11.4 16.3 %collective-permute-start.5 = (bf16[2,64,128]{2,1,0:T(8,128)(2,1)S(1)}, bf16[2,64,128]{2,1,0:T(8,128)(2,1)S(1)}, u32[]{:S(2)}, u32[]{:S(2)}) collective-permute-start(bf16[2,64,128]{2,1,0:T(8,128)(2,1)S(1)} %get-tuple-element.67), channel_id=1, source_target_pairs={{0,496},{16,0},{32,16},{48,32},{64,48},{80,64},{96,80},{112,96},{1... | collective-permute-start | bytes 98312 | tf_op jit(solution)/shard_map/ppermute | solution.py:12
  16.0 11.7 %collective-permute-start.7 = (bf16[2,64,128]{2,1,0:T(8,128)(2,1)S(1)}, bf16[2,64,128]{2,1,0:T(8,128)(2,1)S(1)}, u32[]{:S(2)}, u32[]{:S(2)}) collective-permute-start(bf16[2,64,128]{2,1,0:T(8,128)(2,1)S(1)} %get-tuple-element.68), channel_id=1, source_target_pairs={{0,15},{1,0},{2,1},{3,2},{4,3},{5,4},{6,5},{7,6},{8,7},{9,8},{10,9... | collective-permute-start | bytes 98312 | tf_op jit(solution)/shard_map/ppermute | solution.py:12
  24.8 3.6 copy-start.3
  27.7 2.2 copy-start.7
  30.8 17.3 %collective-permute-start = (bf16[2,64,128]{2,1,0:T(8,128)(2,1)S(1)}, bf16[2,64,128]{2,1,0:T(8,128)(2,1)S(1)}, u32[]{:S(2)}, u32[]{:S(2)}) collective-permute-start(bf16[2,64,128]{2,1,0:T(8,128)(2,1)S(1)} %get-tuple-element.122), channel_id=1, source_target_pairs={{0,15},{1,0},{2,1},{3,2},{4,3},{5,4},{6,5},{7,6},{8,7},{9,8},{10,9... | collective-permute-start | bytes 98312 | tf_op jit(solution)/shard_map/while/body/eval_jaxpr/ppermute | solution.py:12
  34.1 14.0 %collective-permute-start.1 = (bf16[2,64,128]{2,1,0:T(8,128)(2,1)S(1)}, bf16[2,64,128]{2,1,0:T(8,128)(2,1)S(1)}, u32[]{:S(2)}, u32[]{:S(2)}) collective-permute-start(bf16[2,64,128]{2,1,0:T(8,128)(2,1)S(1)} %get-tuple-element.123), channel_id=1, source_target_pairs={{0,1},{1,2},{2,3},{3,4},{4,5},{5,6},{6,7},{7,8},{8,9},{9,10},{10,1... | collective-permute-start | bytes 98312 | tf_op jit(solution)/shard_map/while/body/eval_jaxpr/ppermute | solution.py:12
  36.1 12.1 %collective-permute-start.2 = (bf16[2,64,128]{2,1,0:T(8,128)(2,1)S(1)}, bf16[2,64,128]{2,1,0:T(8,128)(2,1)S(1)}, u32[]{:S(2)}, u32[]{:S(2)}) collective-permute-start(bf16[2,64,128]{2,1,0:T(8,128)(2,1)S(1)} %get-tuple-element.124), channel_id=1, source_target_pairs={{0,496},{16,0},{32,16},{48,32},{64,48},{80,64},{96,80},{112,96},{1... | collective-permute-start | bytes 98312 | tf_op jit(solution)/shard_map/while/body/eval_jaxpr/ppermute | solution.py:12
  42.8 5.4 %collective-permute-start.3 = (bf16[2,64,128]{2,1,0:T(8,128)(2,1)S(1)}, bf16[2,64,128]{2,1,0:T(8,128)(2,1)S(1)}, u32[]{:S(2)}, u32[]{:S(2)}) collective-permute-start(bf16[2,64,128]{2,1,0:T(8,128)(2,1)S(1)} %get-tuple-element.125), channel_id=1, source_target_pairs={{0,16},{16,32},{32,48},{48,64},{64,80},{80,96},{96,112},{112,128},... | collective-permute-start | bytes 98312 | tf_op jit(solution)/shard_map/while/body/eval_jaxpr/ppermute | solution.py:12
  48.8 2.7 copy-start.1
  50.6 1.3 copy-start.4
  52.7 17.2 %collective-permute-start = (bf16[2,64,128]{2,1,0:T(8,128)(2,1)S(1)}, bf16[2,64,128]{2,1,0:T(8,128)(2,1)S(1)}, u32[]{:S(2)}, u32[]{:S(2)}) collective-permute-start(bf16[2,64,128]{2,1,0:T(8,128)(2,1)S(1)} %get-tuple-element.122), channel_id=1, source_target_pairs={{0,15},{1,0},{2,1},{3,2},{4,3},{5,4},{6,5},{7,6},{8,7},{9,8},{10,9... | collective-permute-start | bytes 98312 | tf_op jit(solution)/shard_map/while/body/eval_jaxpr/ppermute | solution.py:12
  57.3 12.7 %collective-permute-start.1 = (bf16[2,64,128]{2,1,0:T(8,128)(2,1)S(1)}, bf16[2,64,128]{2,1,0:T(8,128)(2,1)S(1)}, u32[]{:S(2)}, u32[]{:S(2)}) collective-permute-start(bf16[2,64,128]{2,1,0:T(8,128)(2,1)S(1)} %get-tuple-element.123), channel_id=1, source_target_pairs={{0,1},{1,2},{2,3},{3,4},{4,5},{5,6},{6,7},{7,8},{8,9},{9,10},{10,1... | collective-permute-start | bytes 98312 | tf_op jit(solution)/shard_map/while/body/eval_jaxpr/ppermute | solution.py:12
  59.2 10.7 %collective-permute-start.2 = (bf16[2,64,128]{2,1,0:T(8,128)(2,1)S(1)}, bf16[2,64,128]{2,1,0:T(8,128)(2,1)S(1)}, u32[]{:S(2)}, u32[]{:S(2)}) collective-permute-start(bf16[2,64,128]{2,1,0:T(8,128)(2,1)S(1)} %get-tuple-element.124), channel_id=1, source_target_pairs={{0,496},{16,0},{32,16},{48,32},{64,48},{80,64},{96,80},{112,96},{1... | collective-permute-start | bytes 98312 | tf_op jit(solution)/shard_map/while/body/eval_jaxpr/ppermute | solution.py:12
  64.6 5.4 %collective-permute-start.3 = (bf16[2,64,128]{2,1,0:T(8,128)(2,1)S(1)}, bf16[2,64,128]{2,1,0:T(8,128)(2,1)S(1)}, u32[]{:S(2)}, u32[]{:S(2)}) collective-permute-start(bf16[2,64,128]{2,1,0:T(8,128)(2,1)S(1)} %get-tuple-element.125), channel_id=1, source_target_pairs={{0,16},{16,32},{32,48},{48,64},{64,80},{80,96},{96,112},{112,128},... | collective-permute-start | bytes 98312 | tf_op jit(solution)/shard_map/while/body/eval_jaxpr/ppermute | solution.py:12
  70.6 2.7 copy-start.1
  72.4 1.3 copy-start.4
  74.5 18.8 %collective-permute-start = (bf16[2,64,128]{2,1,0:T(8,128)(2,1)S(1)}, bf16[2,64,128]{2,1,0:T(8,128)(2,1)S(1)}, u32[]{:S(2)}, u32[]{:S(2)}) collective-permute-start(bf16[2,64,128]{2,1,0:T(8,128)(2,1)S(1)} %get-tuple-element.122), channel_id=1, source_target_pairs={{0,15},{1,0},{2,1},{3,2},{4,3},{5,4},{6,5},{7,6},{8,7},{9,8},{10,9... | collective-permute-start | bytes 98312 | tf_op jit(solution)/shard_map/while/body/eval_jaxpr/ppermute | solution.py:12
  79.4 14.0 %collective-permute-start.1 = (bf16[2,64,128]{2,1,0:T(8,128)(2,1)S(1)}, bf16[2,64,128]{2,1,0:T(8,128)(2,1)S(1)}, u32[]{:S(2)}, u32[]{:S(2)}) collective-permute-start(bf16[2,64,128]{2,1,0:T(8,128)(2,1)S(1)} %get-tuple-element.123), channel_id=1, source_target_pairs={{0,1},{1,2},{2,3},{3,4},{4,5},{5,6},{6,7},{7,8},{8,9},{9,10},{10,1... | collective-permute-start | bytes 98312 | tf_op jit(solution)/shard_map/while/body/eval_jaxpr/ppermute | solution.py:12
  81.3 12.0 %collective-permute-start.2 = (bf16[2,64,128]{2,1,0:T(8,128)(2,1)S(1)}, bf16[2,64,128]{2,1,0:T(8,128)(2,1)S(1)}, u32[]{:S(2)}, u32[]{:S(2)}) collective-permute-start(bf16[2,64,128]{2,1,0:T(8,128)(2,1)S(1)} %get-tuple-element.124), channel_id=1, source_target_pairs={{0,496},{16,0},{32,16},{48,32},{64,48},{80,64},{96,80},{112,96},{1... | collective-permute-start | bytes 98312 | tf_op jit(solution)/shard_map/while/body/eval_jaxpr/ppermute | solution.py:12
  88.0 5.4 %collective-permute-start.3 = (bf16[2,64,128]{2,1,0:T(8,128)(2,1)S(1)}, bf16[2,64,128]{2,1,0:T(8,128)(2,1)S(1)}, u32[]{:S(2)}, u32[]{:S(2)}) collective-permute-start(bf16[2,64,128]{2,1,0:T(8,128)(2,1)S(1)} %get-tuple-element.125), channel_id=1, source_target_pairs={{0,16},{16,32},{32,48},{48,64},{64,80},{80,96},{96,112},{112,128},... | collective-permute-start | bytes 98312 | tf_op jit(solution)/shard_map/while/body/eval_jaxpr/ppermute | solution.py:12
  94.0 2.7 copy-start.1
  95.8 1.3 copy-start.4
  97.9 18.8 %collective-permute-start = (bf16[2,64,128]{2,1,0:T(8,128)(2,1)S(1)}, bf16[2,64,128]{2,1,0:T(8,128)(2,1)S(1)}, u32[]{:S(2)}, u32[]{:S(2)}) collective-permute-start(bf16[2,64,128]{2,1,0:T(8,128)(2,1)S(1)} %get-tuple-element.122), channel_id=1, source_target_pairs={{0,15},{1,0},{2,1},{3,2},{4,3},{5,4},{6,5},{7,6},{8,7},{9,8},{10,9... | collective-permute-start | bytes 98312 | tf_op jit(solution)/shard_map/while/body/eval_jaxpr/ppermute | solution.py:12
  102.8 14.0 %collective-permute-start.1 = (bf16[2,64,128]{2,1,0:T(8,128)(2,1)S(1)}, bf16[2,64,128]{2,1,0:T(8,128)(2,1)S(1)}, u32[]{:S(2)}, u32[]{:S(2)}) collective-permute-start(bf16[2,64,128]{2,1,0:T(8,128)(2,1)S(1)} %get-tuple-element.123), channel_id=1, source_target_pairs={{0,1},{1,2},{2,3},{3,4},{4,5},{5,6},{6,7},{7,8},{8,9},{9,10},{10,1... | collective-permute-start | bytes 98312 | tf_op jit(solution)/shard_map/while/body/eval_jaxpr/ppermute | solution.py:12
  104.7 12.0 %collective-permute-start.2 = (bf16[2,64,128]{2,1,0:T(8,128)(2,1)S(1)}, bf16[2,64,128]{2,1,0:T(8,128)(2,1)S(1)}, u32[]{:S(2)}, u32[]{:S(2)}) collective-permute-start(bf16[2,64,128]{2,1,0:T(8,128)(2,1)S(1)} %get-tuple-element.124), channel_id=1, source_target_pairs={{0,496},{16,0},{32,16},{48,32},{64,48},{80,64},{96,80},{112,96},{1... | collective-permute-start | bytes 98312 | tf_op jit(solution)/shard_map/while/body/eval_jaxpr/ppermute | solution.py:12
  111.4 5.4 %collective-permute-start.3 = (bf16[2,64,128]{2,1,0:T(8,128)(2,1)S(1)}, bf16[2,64,128]{2,1,0:T(8,128)(2,1)S(1)}, u32[]{:S(2)}, u32[]{:S(2)}) collective-permute-start(bf16[2,64,128]{2,1,0:T(8,128)(2,1)S(1)} %get-tuple-element.125), channel_id=1, source_target_pairs={{0,16},{16,32},{32,48},{48,64},{64,80},{80,96},{96,112},{112,128},... | collective-permute-start | bytes 98312 | tf_op jit(solution)/shard_map/while/body/eval_jaxpr/ppermute | solution.py:12
  117.4 2.7 copy-start.1
  119.2 1.3 copy-start.4
  121.3 18.8 %collective-permute-start = (bf16[2,64,128]{2,1,0:T(8,128)(2,1)S(1)}, bf16[2,64,128]{2,1,0:T(8,128)(2,1)S(1)}, u32[]{:S(2)}, u32[]{:S(2)}) collective-permute-start(bf16[2,64,128]{2,1,0:T(8,128)(2,1)S(1)} %get-tuple-element.122), channel_id=1, source_target_pairs={{0,15},{1,0},{2,1},{3,2},{4,3},{5,4},{6,5},{7,6},{8,7},{9,8},{10,9... | collective-permute-start | bytes 98312 | tf_op jit(solution)/shard_map/while/body/eval_jaxpr/ppermute | solution.py:12
  126.2 14.0 %collective-permute-start.1 = (bf16[2,64,128]{2,1,0:T(8,128)(2,1)S(1)}, bf16[2,64,128]{2,1,0:T(8,128)(2,1)S(1)}, u32[]{:S(2)}, u32[]{:S(2)}) collective-permute-start(bf16[2,64,128]{2,1,0:T(8,128)(2,1)S(1)} %get-tuple-element.123), channel_id=1, source_target_pairs={{0,1},{1,2},{2,3},{3,4},{4,5},{5,6},{6,7},{7,8},{8,9},{9,10},{10,1... | collective-permute-start | bytes 98312 | tf_op jit(solution)/shard_map/while/body/eval_jaxpr/ppermute | solution.py:12
  128.1 12.0 %collective-permute-start.2 = (bf16[2,64,128]{2,1,0:T(8,128)(2,1)S(1)}, bf16[2,64,128]{2,1,0:T(8,128)(2,1)S(1)}, u32[]{:S(2)}, u32[]{:S(2)}) collective-permute-start(bf16[2,64,128]{2,1,0:T(8,128)(2,1)S(1)} %get-tuple-element.124), channel_id=1, source_target_pairs={{0,496},{16,0},{32,16},{48,32},{64,48},{80,64},{96,80},{112,96},{1... | collective-permute-start | bytes 98312 | tf_op jit(solution)/shard_map/while/body/eval_jaxpr/ppermute | solution.py:12
  134.8 5.4 %collective-permute-start.3 = (bf16[2,64,128]{2,1,0:T(8,128)(2,1)S(1)}, bf16[2,64,128]{2,1,0:T(8,128)(2,1)S(1)}, u32[]{:S(2)}, u32[]{:S(2)}) collective-permute-start(bf16[2,64,128]{2,1,0:T(8,128)(2,1)S(1)} %get-tuple-element.125), channel_id=1, source_target_pairs={{0,16},{16,32},{32,48},{48,64},{64,80},{80,96},{96,112},{112,128},... | collective-permute-start | bytes 98312 | tf_op jit(solution)/shard_map/while/body/eval_jaxpr/ppermute | solution.py:12
  140.8 2.7 copy-start.1
  142.7 1.3 copy-start.4
  144.7 18.8 %collective-permute-start = (bf16[2,64,128]{2,1,0:T(8,128)(2,1)S(1)}, bf16[2,64,128]{2,1,0:T(8,128)(2,1)S(1)}, u32[]{:S(2)}, u32[]{:S(2)}) collective-permute-start(bf16[2,64,128]{2,1,0:T(8,128)(2,1)S(1)} %get-tuple-element.122), channel_id=1, source_target_pairs={{0,15},{1,0},{2,1},{3,2},{4,3},{5,4},{6,5},{7,6},{8,7},{9,8},{10,9... | collective-permute-start | bytes 98312 | tf_op jit(solution)/shard_map/while/body/eval_jaxpr/ppermute | solution.py:12
  149.6 14.0 %collective-permute-start.1 = (bf16[2,64,128]{2,1,0:T(8,128)(2,1)S(1)}, bf16[2,64,128]{2,1,0:T(8,128)(2,1)S(1)}, u32[]{:S(2)}, u32[]{:S(2)}) collective-permute-start(bf16[2,64,128]{2,1,0:T(8,128)(2,1)S(1)} %get-tuple-element.123), channel_id=1, source_target_pairs={{0,1},{1,2},{2,3},{3,4},{4,5},{5,6},{6,7},{7,8},{8,9},{9,10},{10,1... | collective-permute-start | bytes 98312 | tf_op jit(solution)/shard_map/while/body/eval_jaxpr/ppermute | solution.py:12
  151.5 12.0 %collective-permute-start.2 = (bf16[2,64,128]{2,1,0:T(8,128)(2,1)S(1)}, bf16[2,64,128]{2,1,0:T(8,128)(2,1)S(1)}, u32[]{:S(2)}, u32[]{:S(2)}) collective-permute-start(bf16[2,64,128]{2,1,0:T(8,128)(2,1)S(1)} %get-tuple-element.124), channel_id=1, source_target_pairs={{0,496},{16,0},{32,16},{48,32},{64,48},{80,64},{96,80},{112,96},{1... | collective-permute-start | bytes 98312 | tf_op jit(solution)/shard_map/while/body/eval_jaxpr/ppermute | solution.py:12
  158.2 5.4 %collective-permute-start.3 = (bf16[2,64,128]{2,1,0:T(8,128)(2,1)S(1)}, bf16[2,64,128]{2,1,0:T(8,128)(2,1)S(1)}, u32[]{:S(2)}, u32[]{:S(2)}) collective-permute-start(bf16[2,64,128]{2,1,0:T(8,128)(2,1)S(1)} %get-tuple-element.125), channel_id=1, source_target_pairs={{0,16},{16,32},{32,48},{48,64},{64,80},{80,96},{96,112},{112,128},... | collective-permute-start | bytes 98312 | tf_op jit(solution)/shard_map/while/body/eval_jaxpr/ppermute | solution.py:12
  164.2 2.7 copy-start.1
  166.1 1.3 copy-start.4
  168.2 18.8 %collective-permute-start = (bf16[2,64,128]{2,1,0:T(8,128)(2,1)S(1)}, bf16[2,64,128]{2,1,0:T(8,128)(2,1)S(1)}, u32[]{:S(2)}, u32[]{:S(2)}) collective-permute-start(bf16[2,64,128]{2,1,0:T(8,128)(2,1)S(1)} %get-tuple-element.122), channel_id=1, source_target_pairs={{0,15},{1,0},{2,1},{3,2},{4,3},{5,4},{6,5},{7,6},{8,7},{9,8},{10,9... | collective-permute-start | bytes 98312 | tf_op jit(solution)/shard_map/while/body/eval_jaxpr/ppermute | solution.py:12
  173.0 14.0 %collective-permute-start.1 = (bf16[2,64,128]{2,1,0:T(8,128)(2,1)S(1)}, bf16[2,64,128]{2,1,0:T(8,128)(2,1)S(1)}, u32[]{:S(2)}, u32[]{:S(2)}) collective-permute-start(bf16[2,64,128]{2,1,0:T(8,128)(2,1)S(1)} %get-tuple-element.123), channel_id=1, source_target_pairs={{0,1},{1,2},{2,3},{3,4},{4,5},{5,6},{6,7},{7,8},{8,9},{9,10},{10,1... | collective-permute-start | bytes 98312 | tf_op jit(solution)/shard_map/while/body/eval_jaxpr/ppermute | solution.py:12
  174.9 12.0 %collective-permute-start.2 = (bf16[2,64,128]{2,1,0:T(8,128)(2,1)S(1)}, bf16[2,64,128]{2,1,0:T(8,128)(2,1)S(1)}, u32[]{:S(2)}, u32[]{:S(2)}) collective-permute-start(bf16[2,64,128]{2,1,0:T(8,128)(2,1)S(1)} %get-tuple-element.124), channel_id=1, source_target_pairs={{0,496},{16,0},{32,16},{48,32},{64,48},{80,64},{96,80},{112,96},{1... | collective-permute-start | bytes 98312 | tf_op jit(solution)/shard_map/while/body/eval_jaxpr/ppermute | solution.py:12
  181.6 5.4 %collective-permute-start.3 = (bf16[2,64,128]{2,1,0:T(8,128)(2,1)S(1)}, bf16[2,64,128]{2,1,0:T(8,128)(2,1)S(1)}, u32[]{:S(2)}, u32[]{:S(2)}) collective-permute-start(bf16[2,64,128]{2,1,0:T(8,128)(2,1)S(1)} %get-tuple-element.125), channel_id=1, source_target_pairs={{0,16},{16,32},{32,48},{48,64},{64,80},{80,96},{96,112},{112,128},... | collective-permute-start | bytes 98312 | tf_op jit(solution)/shard_map/while/body/eval_jaxpr/ppermute | solution.py:12
  187.6 2.7 copy-start.1
  189.5 1.3 copy-start.4
  191.6 18.8 %collective-permute-start = (bf16[2,64,128]{2,1,0:T(8,128)(2,1)S(1)}, bf16[2,64,128]{2,1,0:T(8,128)(2,1)S(1)}, u32[]{:S(2)}, u32[]{:S(2)}) collective-permute-start(bf16[2,64,128]{2,1,0:T(8,128)(2,1)S(1)} %get-tuple-element.122), channel_id=1, source_target_pairs={{0,15},{1,0},{2,1},{3,2},{4,3},{5,4},{6,5},{7,6},{8,7},{9,8},{10,9... | collective-permute-start | bytes 98312 | tf_op jit(solution)/shard_map/while/body/eval_jaxpr/ppermute | solution.py:12
  196.4 14.0 %collective-permute-start.1 = (bf16[2,64,128]{2,1,0:T(8,128)(2,1)S(1)}, bf16[2,64,128]{2,1,0:T(8,128)(2,1)S(1)}, u32[]{:S(2)}, u32[]{:S(2)}) collective-permute-start(bf16[2,64,128]{2,1,0:T(8,128)(2,1)S(1)} %get-tuple-element.123), channel_id=1, source_target_pairs={{0,1},{1,2},{2,3},{3,4},{4,5},{5,6},{6,7},{7,8},{8,9},{9,10},{10,1... | collective-permute-start | bytes 98312 | tf_op jit(solution)/shard_map/while/body/eval_jaxpr/ppermute | solution.py:12
  198.3 12.0 %collective-permute-start.2 = (bf16[2,64,128]{2,1,0:T(8,128)(2,1)S(1)}, bf16[2,64,128]{2,1,0:T(8,128)(2,1)S(1)}, u32[]{:S(2)}, u32[]{:S(2)}) collective-permute-start(bf16[2,64,128]{2,1,0:T(8,128)(2,1)S(1)} %get-tuple-element.124), channel_id=1, source_target_pairs={{0,496},{16,0},{32,16},{48,32},{64,48},{80,64},{96,80},{112,96},{1... | collective-permute-start | bytes 98312 | tf_op jit(solution)/shard_map/while/body/eval_jaxpr/ppermute | solution.py:12
  205.0 5.4 %collective-permute-start.3 = (bf16[2,64,128]{2,1,0:T(8,128)(2,1)S(1)}, bf16[2,64,128]{2,1,0:T(8,128)(2,1)S(1)}, u32[]{:S(2)}, u32[]{:S(2)}) collective-permute-start(bf16[2,64,128]{2,1,0:T(8,128)(2,1)S(1)} %get-tuple-element.125), channel_id=1, source_target_pairs={{0,16},{16,32},{32,48},{48,64},{64,80},{80,96},{96,112},{112,128},... | collective-permute-start | bytes 98312 | tf_op jit(solution)/shard_map/while/body/eval_jaxpr/ppermute | solution.py:12
  211.0 2.7 copy-start.1
  212.9 1.3 copy-start.4
  319.6 99.8 %copy-start.5 = (f32[16,64,128]{2,1,0:T(8,128)}, f32[16,64,128]{2,1,0:T(8,128)S(1)}, u32[]{:S(2)}) copy-start(f32[16,64,128]{2,1,0:T(8,128)S(1)} %broadcast_multiply_fusion) | copy-start | bytes 1572868
where the time goes:
time: 421 us; the launch traced here: 419 us
  blocking collectives  204 us (48%)
  starting transfers between devices  139 us (33%)
  matrix products  38.8 us (9%)
  local copies, waits for them, and re-layouts  32.5 us (8%)
    ppermute x36, starting transfers between devices, from_behind(): return lax.ppermute(value, axis, pairs)  139 us
    psum x1, blocking collectives, shards(): squares = lax.psum(jnp.sum(current * current, axis=(0, 2)), ('px', 'py'))  105 us
    psum x1, blocking collectives, shards(): gram_matrix = lax.psum(partial_gram, ('px', 'py')) / total_rows  98.6 us
    dot_general x9, matrix products, operator_apply(): jnp.einsum('rtkj,rtij->rki', gathered, local_tiles, preferred_element_typ...  22.3 us
    dot_general x9, matrix products, operator_apply(): jnp.einsum('rkj,rij->rki', received[halo_slot], halo_tiles, preferred_ele...  16 us
    while x48, local copies, waits for them, and re-layouts  9.86 us
  transfers between devices with their start and end apart: 36, of which 0 were waited for; matrix products, arithmetic and copies ran while one was open for 8% of the time, Pallas kernels for 0%

commit v1 on v0

--- a/solution.py
+++ b/solution.py
@@ -43,7 +43,7 @@
 
     previous, current = lax.fori_loop(0, DEG - 1, advance, (start_vecs, first_vecs))
     total_rows = current.shape[0] * current.shape[2] * lax.axis_size("px") * lax.axis_size("py")
-    squares = lax.psum(jnp.sum(current * current, axis=(0, 2)), ("px", "py"))
+    squares = jnp.sum(lax.all_gather(jnp.sum(current * current, axis=(0, 2)), ("px", "py")), axis=0)
     scales = lax.rsqrt(squares / total_rows + 1e-06)
     filtered = current * scales[None, :, None]
     partial_gram = jnp.einsum("rkj,rlj->kl", filtered, filtered, precision=lax.Precision.HIGHEST)

time: 421 us -> 787 us (1.87)
  waiting for transfers between devices: 0.09 us -> 454 us
  blocking collectives: 204 us -> 99.8 us
  between operations: 0.85 us -> 14.3 us
    unnamed x0 -> x2, waiting for transfers between devices: none -> 454 us
    psum x1 -> x0, blocking collectives: 105 us -> none  [shards(): squares = lax.psum(jnp.sum(current * current, axis=(0, 2)), ('px', 'py'))]
  transfers between devices with their start and end apart: 36 -> 37, of which waited for: 0 -> 1; matrix products, arithmetic and copies ran while one was open for 8% -> 4% of each run, Pallas kernels for 0% -> 0%
where the time goes in v1:
time: 787 us; the launch traced here: 785 us
  waiting for transfers between devices  454 us (58%)
  starting transfers between devices  140 us (18%)
  blocking collectives  99.8 us (13%)
  matrix products  38.8 us (5%)
  local copies, waits for them, and re-layouts  34.4 us (4%)
  between operations  14.3 us (2%)
    unnamed x2, waiting for transfers between devices  454 us
    ppermute x36, starting transfers between devices, from_behind(): return lax.ppermute(value, axis, pairs)  140 us
    psum x1, blocking collectives, shards(): gram_matrix = lax.psum(partial_gram, ('px', 'py')) / total_rows  99.8 us
    dot_general x9, matrix products, operator_apply(): jnp.einsum('rtkj,rtij->rki', gathered, local_tiles, preferred_element_typ...  22.2 us
    dot_general x9, matrix products, operator_apply(): jnp.einsum('rkj,rij->rki', received[halo_slot], halo_tiles, preferred_ele...  16 us
  transfers between devices with their start and end apart: 37, of which 1 were waited for; matrix products, arithmetic and copies ran while one was open for 4% of the time, Pallas kernels for 0%

profile of v1, /device:TPU:1, one launch (start us, length us, event | category | flops | bytes accessed | tf_op | source)
XLA Modules:
  0.0 785.4 jit_solution(10212264804263700301)
XLA Ops:
  7.2 1.2 copy.35
  10.0 4.5 collective-permute-start.4
  14.5 6.2 collective-permute-start.5
  20.7 1.9 collective-permute-start.6
  22.6 6.9 collective-permute-start.7
  29.7 1.7 gather_fusion.3
  31.4 2.9 convolution_bitcast_fusion.1
  35.0 1.5 convolution_add_fusion.1
  36.5 184.5 %while.12 = (s32[]{:T(128)}, f32[16,64,128]{2,1,0:T(8,128)}, f32[16,64,128]{2,1,0:T(8,128)S(1)}, s32[16,4]{0,1:T(4,128)S(1)}, bf16[16,4,128,128]{3,2,1,0:T(8,128...) while((s32[]{:T(128)}, f32[16,64,128]{2,1,0:T(8,128)}, ...), condition=%wide.region_1.0_spmd, body=%wide.region_0.0_spmd.sunk | while | flops 168496400 | bytes 23345988 | solution.py:44
  37.4 3.4 collective-permute-start
  40.7 1.9 collective-permute-start.1
  42.7 6.7 collective-permute-start.2
  49.4 1.9 collective-permute-start.3
  52.3 2.4 convolution_bitcast_fusion.4
  55.4 1.8 fusion.28
  57.2 0.8 copy.29
  59.3 4.9 collective-permute-start
  64.2 1.9 collective-permute-start.1
  66.1 5.4 collective-permute-start.2
  71.5 1.9 collective-permute-start.3
  74.4 2.4 convolution_bitcast_fusion.4
  77.5 1.8 fusion.28
  79.3 0.8 copy.29
  81.4 4.9 collective-permute-start
  86.3 1.9 collective-permute-start.1
  88.2 6.7 collective-permute-start.2
  94.9 1.9 collective-permute-start.3
  97.8 2.4 convolution_bitcast_fusion.4
  100.9 1.8 fusion.28
  104.8 4.9 collective-permute-start
  109.7 1.9 collective-permute-start.1
  111.6 6.7 collective-permute-start.2
  118.3 1.9 collective-permute-start.3
  121.2 2.4 convolution_bitcast_fusion.4
  124.3 1.8 fusion.28
  128.2 4.9 collective-permute-start
  133.1 1.9 collective-permute-start.1
  135.0 6.7 collective-permute-start.2
  141.7 1.9 collective-permute-start.3
  144.6 2.4 convolution_bitcast_fusion.4
  147.7 1.8 fusion.28
  149.6 0.8 copy.29
  151.6 4.9 collective-permute-start
  156.5 1.9 collective-permute-start.1
  158.4 6.7 collective-permute-start.2
  165.1 1.9 collective-permute-start.3
  168.0 2.4 convolution_bitcast_fusion.4
  171.1 1.8 fusion.28
  175.1 4.9 collective-permute-start
  179.9 1.9 collective-permute-start.1
  181.8 6.7 collective-permute-start.2
  188.5 1.9 collective-permute-start.3
  191.4 2.4 convolution_bitcast_fusion.4
  194.5 1.8 fusion.28
  198.5 4.9 collective-permute-start
  203.3 1.9 collective-permute-start.1
  205.3 6.7 collective-permute-start.2
  211.9 1.9 collective-permute-start.3
  214.8 2.4 convolution_bitcast_fusion.4
  218.0 1.8 fusion.28
  219.8 0.8 copy.29
  222.1 454.2 %all-reduce.3.cloned.1.call-done = f32[32768]{0:T(1024)} async-done(((f32[32768]{0:T(1024)}), f32[32768]{0:T(1024)}) %all-reduce.3.cloned.1.call-update) | async-done | bytes 131088
  676.4 1.0 reshape.102
  678.2 99.8 %psum.7 = f32[64,64]{1,0:T(8,128)S(1)} all-reduce(f32[64,64]{1,0:T(8,128)S(1)} %convolution_bitcast_fusion.2), channel_id=1, replica_groups=mesh['px'=32,'py'=16] {'px','py'}, use_global_device_ids=true, to_apply=%region_4.0 | all-reduce | flops 4096 | bytes 32768 | tf_op jit(solution)/shard_map/psum | solution.py:50
  (249 shorter events, 30.6 us)
Async XLA Ops:
  7.2 24.2 %copy-start = (bf16[16,4,128,128]{3,2,1,0:T(8,128)(2,1)S(1)}, bf16[16,4,128,128]{3,2,1,0:T(8,128)(2,1)}, u32[]{:S(2)}) copy-start(bf16[16,4,128,128]{3,2,1,0:T(8,128)(2,1)} %param.9) | copy-start | bytes 6291460
  7.2 22.3 %copy-start.7 = (s32[16,4]{0,1:T(4,128)S(1)}, s32[16,4]{0,1:T(4,128)}, u32[]{:S(2)}) copy-start(s32[16,4]{0,1:T(4,128)} %param.10) | copy-start | bytes 772
  7.2 22.3 %copy-start.9 = (s32[16]{0:T(128)S(1)}, s32[16]{0:T(128)}, u32[]{:S(2)}) copy-start(s32[16]{0:T(128)} %param.12) | copy-start | bytes 196
  7.2 669.2 %all-reduce.3.cloned.1.call-start = ((), (), s32[]{:S(2)}) async-start(), calls=%async_computation | async-start | bytes 262144
  8.4 25.9 %copy-start.2 = (f32[16,64,128]{2,1,0:T(8,128)}, f32[16,64,128]{2,1,0:T(8,128)S(1)}, u32[]{:S(2)}) copy-start(f32[16,64,128]{2,1,0:T(8,128)S(1)} %copy.35) | copy-start | bytes 1572868
  10.0 24.3 %collective-permute-start.4 = (bf16[2,64,128]{2,1,0:T(8,128)(2,1)S(1)}, bf16[2,64,128]{2,1,0:T(8,128)(2,1)S(1)}, u32[]{:S(2)}, u32[]{:S(2)}) collective-permute-start(bf16[2,64,128]{2,1,0:T(8,128)(2,1)S(1)} %get-tuple-element.65), channel_id=1, source_target_pairs={{0,16},{16,32},{32,48},{48,64},{64,80},{80,96},{96,112},{112,128},... | collective-permute-start | bytes 98312 | tf_op jit(solution)/shard_map/ppermute | solution.py:12
  14.5 19.8 %collective-permute-start.5 = (bf16[2,64,128]{2,1,0:T(8,128)(2,1)S(1)}, bf16[2,64,128]{2,1,0:T(8,128)(2,1)S(1)}, u32[]{:S(2)}, u32[]{:S(2)}) collective-permute-start(bf16[2,64,128]{2,1,0:T(8,128)(2,1)S(1)} %get-tuple-element.67), channel_id=1, source_target_pairs={{0,496},{16,0},{32,16},{48,32},{64,48},{80,64},{96,80},{112,96},{1... | collective-permute-start | bytes 98312 | tf_op jit(solution)/shard_map/ppermute | solution.py:12
  20.7 13.7 %collective-permute-start.6 = (bf16[2,64,128]{2,1,0:T(8,128)(2,1)S(1)}, bf16[2,64,128]{2,1,0:T(8,128)(2,1)S(1)}, u32[]{:S(2)}, u32[]{:S(2)}) collective-permute-start(bf16[2,64,128]{2,1,0:T(8,128)(2,1)S(1)} %get-tuple-element.66), channel_id=1, source_target_pairs={{0,1},{1,2},{2,3},{3,4},{4,5},{5,6},{6,7},{7,8},{8,9},{9,10},{10,1... | collective-permute-start | bytes 98312 | tf_op jit(solution)/shard_map/ppermute | solution.py:12
  22.6 11.8 %collective-permute-start.7 = (bf16[2,64,128]{2,1,0:T(8,128)(2,1)S(1)}, bf16[2,64,128]{2,1,0:T(8,128)(2,1)S(1)}, u32[]{:S(2)}, u32[]{:S(2)}) collective-permute-start(bf16[2,64,128]{2,1,0:T(8,128)(2,1)S(1)} %get-tuple-element.68), channel_id=1, source_target_pairs={{0,15},{1,0},{2,1},{3,2},{4,3},{5,4},{6,5},{7,6},{8,7},{9,8},{10,9... | collective-permute-start | bytes 98312 | tf_op jit(solution)/shard_map/ppermute | solution.py:12
  31.4 3.6 copy-start.3
  34.3 2.2 copy-start.8
  37.4 17.3 %collective-permute-start = (bf16[2,64,128]{2,1,0:T(8,128)(2,1)S(1)}, bf16[2,64,128]{2,1,0:T(8,128)(2,1)S(1)}, u32[]{:S(2)}, u32[]{:S(2)}) collective-permute-start(bf16[2,64,128]{2,1,0:T(8,128)(2,1)S(1)} %get-tuple-element.122), channel_id=1, source_target_pairs={{0,15},{1,0},{2,1},{3,2},{4,3},{5,4},{6,5},{7,6},{8,7},{9,8},{10,9... | collective-permute-start | bytes 98312 | tf_op jit(solution)/shard_map/while/body/eval_jaxpr/ppermute | solution.py:12
  40.7 14.0 %collective-permute-start.1 = (bf16[2,64,128]{2,1,0:T(8,128)(2,1)S(1)}, bf16[2,64,128]{2,1,0:T(8,128)(2,1)S(1)}, u32[]{:S(2)}, u32[]{:S(2)}) collective-permute-start(bf16[2,64,128]{2,1,0:T(8,128)(2,1)S(1)} %get-tuple-element.123), channel_id=1, source_target_pairs={{0,1},{1,2},{2,3},{3,4},{4,5},{5,6},{6,7},{7,8},{8,9},{9,10},{10,1... | collective-permute-start | bytes 98312 | tf_op jit(solution)/shard_map/while/body/eval_jaxpr/ppermute | solution.py:12
  42.7 12.1 %collective-permute-start.2 = (bf16[2,64,128]{2,1,0:T(8,128)(2,1)S(1)}, bf16[2,64,128]{2,1,0:T(8,128)(2,1)S(1)}, u32[]{:S(2)}, u32[]{:S(2)}) collective-permute-start(bf16[2,64,128]{2,1,0:T(8,128)(2,1)S(1)} %get-tuple-element.124), channel_id=1, source_target_pairs={{0,496},{16,0},{32,16},{48,32},{64,48},{80,64},{96,80},{112,96},{1... | collective-permute-start | bytes 98312 | tf_op jit(solution)/shard_map/while/body/eval_jaxpr/ppermute | solution.py:12
  49.4 5.4 collective-permute-start.3
  55.4 2.7 copy-start.1
  57.2 1.3 copy-start.4
  59.3 17.5 %collective-permute-start = (bf16[2,64,128]{2,1,0:T(8,128)(2,1)S(1)}, bf16[2,64,128]{2,1,0:T(8,128)(2,1)S(1)}, u32[]{:S(2)}, u32[]{:S(2)}) collective-permute-start(bf16[2,64,128]{2,1,0:T(8,128)(2,1)S(1)} %get-tuple-element.122), channel_id=1, source_target_pairs={{0,15},{1,0},{2,1},{3,2},{4,3},{5,4},{6,5},{7,6},{8,7},{9,8},{10,9... | collective-permute-start | bytes 98312 | tf_op jit(solution)/shard_map/while/body/eval_jaxpr/ppermute | solution.py:12
  64.2 12.7 %collective-permute-start.1 = (bf16[2,64,128]{2,1,0:T(8,128)(2,1)S(1)}, bf16[2,64,128]{2,1,0:T(8,128)(2,1)S(1)}, u32[]{:S(2)}, u32[]{:S(2)}) collective-permute-start(bf16[2,64,128]{2,1,0:T(8,128)(2,1)S(1)} %get-tuple-element.123), channel_id=1, source_target_pairs={{0,1},{1,2},{2,3},{3,4},{4,5},{5,6},{6,7},{7,8},{8,9},{9,10},{10,1... | collective-permute-start | bytes 98312 | tf_op jit(solution)/shard_map/while/body/eval_jaxpr/ppermute | solution.py:12
  66.1 10.7 %collective-permute-start.2 = (bf16[2,64,128]{2,1,0:T(8,128)(2,1)S(1)}, bf16[2,64,128]{2,1,0:T(8,128)(2,1)S(1)}, u32[]{:S(2)}, u32[]{:S(2)}) collective-permute-start(bf16[2,64,128]{2,1,0:T(8,128)(2,1)S(1)} %get-tuple-element.124), channel_id=1, source_target_pairs={{0,496},{16,0},{32,16},{48,32},{64,48},{80,64},{96,80},{112,96},{1... | collective-permute-start | bytes 98312 | tf_op jit(solution)/shard_map/while/body/eval_jaxpr/ppermute | solution.py:12
  71.5 5.4 collective-permute-start.3
  77.5 2.7 copy-start.1
  79.3 1.3 copy-start.4
  81.4 18.8 %collective-permute-start = (bf16[2,64,128]{2,1,0:T(8,128)(2,1)S(1)}, bf16[2,64,128]{2,1,0:T(8,128)(2,1)S(1)}, u32[]{:S(2)}, u32[]{:S(2)}) collective-permute-start(bf16[2,64,128]{2,1,0:T(8,128)(2,1)S(1)} %get-tuple-element.122), channel_id=1, source_target_pairs={{0,15},{1,0},{2,1},{3,2},{4,3},{5,4},{6,5},{7,6},{8,7},{9,8},{10,9... | collective-permute-start | bytes 98312 | tf_op jit(solution)/shard_map/while/body/eval_jaxpr/ppermute | solution.py:12
  86.3 14.0 %collective-permute-start.1 = (bf16[2,64,128]{2,1,0:T(8,128)(2,1)S(1)}, bf16[2,64,128]{2,1,0:T(8,128)(2,1)S(1)}, u32[]{:S(2)}, u32[]{:S(2)}) collective-permute-start(bf16[2,64,128]{2,1,0:T(8,128)(2,1)S(1)} %get-tuple-element.123), channel_id=1, source_target_pairs={{0,1},{1,2},{2,3},{3,4},{4,5},{5,6},{6,7},{7,8},{8,9},{9,10},{10,1... | collective-permute-start | bytes 98312 | tf_op jit(solution)/shard_map/while/body/eval_jaxpr/ppermute | solution.py:12
  88.2 12.0 %collective-permute-start.2 = (bf16[2,64,128]{2,1,0:T(8,128)(2,1)S(1)}, bf16[2,64,128]{2,1,0:T(8,128)(2,1)S(1)}, u32[]{:S(2)}, u32[]{:S(2)}) collective-permute-start(bf16[2,64,128]{2,1,0:T(8,128)(2,1)S(1)} %get-tuple-element.124), channel_id=1, source_target_pairs={{0,496},{16,0},{32,16},{48,32},{64,48},{80,64},{96,80},{112,96},{1... | collective-permute-start | bytes 98312 | tf_op jit(solution)/shard_map/while/body/eval_jaxpr/ppermute | solution.py:12
  94.9 5.4 collective-permute-start.3
  100.9 2.7 copy-start.1
  102.7 1.3 copy-start.4
  104.8 18.8 %collective-permute-start = (bf16[2,64,128]{2,1,0:T(8,128)(2,1)S(1)}, bf16[2,64,128]{2,1,0:T(8,128)(2,1)S(1)}, u32[]{:S(2)}, u32[]{:S(2)}) collective-permute-start(bf16[2,64,128]{2,1,0:T(8,128)(2,1)S(1)} %get-tuple-element.122), channel_id=1, source_target_pairs={{0,15},{1,0},{2,1},{3,2},{4,3},{5,4},{6,5},{7,6},{8,7},{9,8},{10,9... | collective-permute-start | bytes 98312 | tf_op jit(solution)/shard_map/while/body/eval_jaxpr/ppermute | solution.py:12
  109.7 14.0 %collective-permute-start.1 = (bf16[2,64,128]{2,1,0:T(8,128)(2,1)S(1)}, bf16[2,64,128]{2,1,0:T(8,128)(2,1)S(1)}, u32[]{:S(2)}, u32[]{:S(2)}) collective-permute-start(bf16[2,64,128]{2,1,0:T(8,128)(2,1)S(1)} %get-tuple-element.123), channel_id=1, source_target_pairs={{0,1},{1,2},{2,3},{3,4},{4,5},{5,6},{6,7},{7,8},{8,9},{9,10},{10,1... | collective-permute-start | bytes 98312 | tf_op jit(solution)/shard_map/while/body/eval_jaxpr/ppermute | solution.py:12
  111.6 12.0 %collective-permute-start.2 = (bf16[2,64,128]{2,1,0:T(8,128)(2,1)S(1)}, bf16[2,64,128]{2,1,0:T(8,128)(2,1)S(1)}, u32[]{:S(2)}, u32[]{:S(2)}) collective-permute-start(bf16[2,64,128]{2,1,0:T(8,128)(2,1)S(1)} %get-tuple-element.124), channel_id=1, source_target_pairs={{0,496},{16,0},{32,16},{48,32},{64,48},{80,64},{96,80},{112,96},{1... | collective-permute-start | bytes 98312 | tf_op jit(solution)/shard_map/while/body/eval_jaxpr/ppermute | solution.py:12
  118.3 5.4 collective-permute-start.3
  124.3 2.7 copy-start.1
  126.1 1.3 copy-start.4
  128.2 18.8 %collective-permute-start = (bf16[2,64,128]{2,1,0:T(8,128)(2,1)S(1)}, bf16[2,64,128]{2,1,0:T(8,128)(2,1)S(1)}, u32[]{:S(2)}, u32[]{:S(2)}) collective-permute-start(bf16[2,64,128]{2,1,0:T(8,128)(2,1)S(1)} %get-tuple-element.122), channel_id=1, source_target_pairs={{0,15},{1,0},{2,1},{3,2},{4,3},{5,4},{6,5},{7,6},{8,7},{9,8},{10,9... | collective-permute-start | bytes 98312 | tf_op jit(solution)/shard_map/while/body/eval_jaxpr/ppermute | solution.py:12
  133.1 14.0 %collective-permute-start.1 = (bf16[2,64,128]{2,1,0:T(8,128)(2,1)S(1)}, bf16[2,64,128]{2,1,0:T(8,128)(2,1)S(1)}, u32[]{:S(2)}, u32[]{:S(2)}) collective-permute-start(bf16[2,64,128]{2,1,0:T(8,128)(2,1)S(1)} %get-tuple-element.123), channel_id=1, source_target_pairs={{0,1},{1,2},{2,3},{3,4},{4,5},{5,6},{6,7},{7,8},{8,9},{9,10},{10,1... | collective-permute-start | bytes 98312 | tf_op jit(solution)/shard_map/while/body/eval_jaxpr/ppermute | solution.py:12
  135.0 12.0 %collective-permute-start.2 = (bf16[2,64,128]{2,1,0:T(8,128)(2,1)S(1)}, bf16[2,64,128]{2,1,0:T(8,128)(2,1)S(1)}, u32[]{:S(2)}, u32[]{:S(2)}) collective-permute-start(bf16[2,64,128]{2,1,0:T(8,128)(2,1)S(1)} %get-tuple-element.124), channel_id=1, source_target_pairs={{0,496},{16,0},{32,16},{48,32},{64,48},{80,64},{96,80},{112,96},{1... | collective-permute-start | bytes 98312 | tf_op jit(solution)/shard_map/while/body/eval_jaxpr/ppermute | solution.py:12
  141.7 5.4 collective-permute-start.3
  147.7 2.7 copy-start.1
  149.5 1.3 copy-start.4
  151.6 18.8 %collective-permute-start = (bf16[2,64,128]{2,1,0:T(8,128)(2,1)S(1)}, bf16[2,64,128]{2,1,0:T(8,128)(2,1)S(1)}, u32[]{:S(2)}, u32[]{:S(2)}) collective-permute-start(bf16[2,64,128]{2,1,0:T(8,128)(2,1)S(1)} %get-tuple-element.122), channel_id=1, source_target_pairs={{0,15},{1,0},{2,1},{3,2},{4,3},{5,4},{6,5},{7,6},{8,7},{9,8},{10,9... | collective-permute-start | bytes 98312 | tf_op jit(solution)/shard_map/while/body/eval_jaxpr/ppermute | solution.py:12
  156.5 14.0 %collective-permute-start.1 = (bf16[2,64,128]{2,1,0:T(8,128)(2,1)S(1)}, bf16[2,64,128]{2,1,0:T(8,128)(2,1)S(1)}, u32[]{:S(2)}, u32[]{:S(2)}) collective-permute-start(bf16[2,64,128]{2,1,0:T(8,128)(2,1)S(1)} %get-tuple-element.123), channel_id=1, source_target_pairs={{0,1},{1,2},{2,3},{3,4},{4,5},{5,6},{6,7},{7,8},{8,9},{9,10},{10,1... | collective-permute-start | bytes 98312 | tf_op jit(solution)/shard_map/while/body/eval_jaxpr/ppermute | solution.py:12
  158.4 12.0 %collective-permute-start.2 = (bf16[2,64,128]{2,1,0:T(8,128)(2,1)S(1)}, bf16[2,64,128]{2,1,0:T(8,128)(2,1)S(1)}, u32[]{:S(2)}, u32[]{:S(2)}) collective-permute-start(bf16[2,64,128]{2,1,0:T(8,128)(2,1)S(1)} %get-tuple-element.124), channel_id=1, source_target_pairs={{0,496},{16,0},{32,16},{48,32},{64,48},{80,64},{96,80},{112,96},{1... | collective-permute-start | bytes 98312 | tf_op jit(solution)/shard_map/while/body/eval_jaxpr/ppermute | solution.py:12
  165.1 5.4 collective-permute-start.3
  171.1 2.7 copy-start.1
  173.0 1.3 copy-start.4
  175.1 18.8 %collective-permute-start = (bf16[2,64,128]{2,1,0:T(8,128)(2,1)S(1)}, bf16[2,64,128]{2,1,0:T(8,128)(2,1)S(1)}, u32[]{:S(2)}, u32[]{:S(2)}) collective-permute-start(bf16[2,64,128]{2,1,0:T(8,128)(2,1)S(1)} %get-tuple-element.122), channel_id=1, source_target_pairs={{0,15},{1,0},{2,1},{3,2},{4,3},{5,4},{6,5},{7,6},{8,7},{9,8},{10,9... | collective-permute-start | bytes 98312 | tf_op jit(solution)/shard_map/while/body/eval_jaxpr/ppermute | solution.py:12
  179.9 14.0 %collective-permute-start.1 = (bf16[2,64,128]{2,1,0:T(8,128)(2,1)S(1)}, bf16[2,64,128]{2,1,0:T(8,128)(2,1)S(1)}, u32[]{:S(2)}, u32[]{:S(2)}) collective-permute-start(bf16[2,64,128]{2,1,0:T(8,128)(2,1)S(1)} %get-tuple-element.123), channel_id=1, source_target_pairs={{0,1},{1,2},{2,3},{3,4},{4,5},{5,6},{6,7},{7,8},{8,9},{9,10},{10,1... | collective-permute-start | bytes 98312 | tf_op jit(solution)/shard_map/while/body/eval_jaxpr/ppermute | solution.py:12
  181.8 12.0 %collective-permute-start.2 = (bf16[2,64,128]{2,1,0:T(8,128)(2,1)S(1)}, bf16[2,64,128]{2,1,0:T(8,128)(2,1)S(1)}, u32[]{:S(2)}, u32[]{:S(2)}) collective-permute-start(bf16[2,64,128]{2,1,0:T(8,128)(2,1)S(1)} %get-tuple-element.124), channel_id=1, source_target_pairs={{0,496},{16,0},{32,16},{48,32},{64,48},{80,64},{96,80},{112,96},{1... | collective-permute-start | bytes 98312 | tf_op jit(solution)/shard_map/while/body/eval_jaxpr/ppermute | solution.py:12
  188.5 5.4 collective-permute-start.3
  194.5 2.7 copy-start.1
  196.4 1.3 copy-start.4
  198.5 18.8 %collective-permute-start = (bf16[2,64,128]{2,1,0:T(8,128)(2,1)S(1)}, bf16[2,64,128]{2,1,0:T(8,128)(2,1)S(1)}, u32[]{:S(2)}, u32[]{:S(2)}) collective-permute-start(bf16[2,64,128]{2,1,0:T(8,128)(2,1)S(1)} %get-tuple-element.122), channel_id=1, source_target_pairs={{0,15},{1,0},{2,1},{3,2},{4,3},{5,4},{6,5},{7,6},{8,7},{9,8},{10,9... | collective-permute-start | bytes 98312 | tf_op jit(solution)/shard_map/while/body/eval_jaxpr/ppermute | solution.py:12
  203.3 14.0 %collective-permute-start.1 = (bf16[2,64,128]{2,1,0:T(8,128)(2,1)S(1)}, bf16[2,64,128]{2,1,0:T(8,128)(2,1)S(1)}, u32[]{:S(2)}, u32[]{:S(2)}) collective-permute-start(bf16[2,64,128]{2,1,0:T(8,128)(2,1)S(1)} %get-tuple-element.123), channel_id=1, source_target_pairs={{0,1},{1,2},{2,3},{3,4},{4,5},{5,6},{6,7},{7,8},{8,9},{9,10},{10,1... | collective-permute-start | bytes 98312 | tf_op jit(solution)/shard_map/while/body/eval_jaxpr/ppermute | solution.py:12
  205.3 12.0 %collective-permute-start.2 = (bf16[2,64,128]{2,1,0:T(8,128)(2,1)S(1)}, bf16[2,64,128]{2,1,0:T(8,128)(2,1)S(1)}, u32[]{:S(2)}, u32[]{:S(2)}) collective-permute-start(bf16[2,64,128]{2,1,0:T(8,128)(2,1)S(1)} %get-tuple-element.124), channel_id=1, source_target_pairs={{0,496},{16,0},{32,16},{48,32},{64,48},{80,64},{96,80},{112,96},{1... | collective-permute-start | bytes 98312 | tf_op jit(solution)/shard_map/while/body/eval_jaxpr/ppermute | solution.py:12
  211.9 5.4 collective-permute-start.3
  217.9 2.7 copy-start.1
  219.8 1.3 copy-start.4
  221.5 0.7 copy-start.6
  677.6 101.0 %copy-start.5 = (f32[16,64,128]{2,1,0:T(8,128)}, f32[16,64,128]{2,1,0:T(8,128)S(1)}, u32[]{:S(2)}) copy-start(f32[16,64,128]{2,1,0:T(8,128)S(1)} %broadcast_multiply_fusion) | copy-start | bytes 1572868
Sparse Core Ops, SparseCore 0:
  222.3 454.0 all-reduce.2
